TPU v7x, 256 devices: a whole 4x4x8 slice. The times are simulated.
256 devices in a mesh: tm: 16 (over z, core), head: 16 (over y, x).
Axes of the slice: x: 4, y: 4, z: 8, core: 2. Of those that a mesh axis runs over, the one named last changes fastest.
Arguments:
- frames: bfloat16 [8192, 2048], P(('tm', 'head')), may hold values from -6 to 6
- log_decay: float32 [8192, 16], P('tm', 'head'), may hold values from -2 to 0, as said below
- w_query: bfloat16 [2048, 2048], P('tm', 'head'), may hold values from -0.125 to 0.125
- w_key: bfloat16 [2048, 2048], P('tm', 'head'), may hold values from -0.125 to 0.125
- w_value: bfloat16 [2048, 2048], P('tm', 'head'), may hold values from -0.125 to 0.125
- w_gate: bfloat16 [2048, 2048], P('tm', 'head'), may hold values from -0.125 to 0.125
- w_out: bfloat16 [2048, 2048], P('head', 'tm'), may hold values from -0.125 to 0.125
Outputs:
- mixed: bfloat16 [8192, 2048], P(('tm', 'head'))
Inputs may be any that keep to these rules, and one draw needn't show every extreme that they name: `log_decay`: strictly negative.
All inputs are finite; a program needn't handle non-finite values.
Results may differ from a plain program's by a relative error of at most 0.015.
Values may be sent and summed in bfloat16 or wider, within the bound.
No kernel may reach another device: no remote copies, remote signals or barrier semaphores. Data moves between devices by JAX's collectives and lax.ppermute only.
A program may use at most 64 MiB of HBM per device.

v0:
```python
import jax
import jax.numpy as jnp
from jax import lax
from jax.sharding import PartitionSpec as P

HEAD_DIM = 128
BLOCK = 512
PAD_ROWS = 8


def gather_by_exchange(part, axis):
    count = lax.axis_size(axis)
    copies = jnp.broadcast_to(part[None], (count,) + part.shape)
    return lax.all_to_all(copies, axis, 0, 0, tiled=False)


def prior_state(local_final, log_total, axis):
    heads_here = local_final.shape[0]
    high = log_total.astype(jnp.bfloat16)
    low = (log_total - high.astype(jnp.float32)).astype(jnp.bfloat16)
    extra = jnp.concatenate(
        [
            jnp.broadcast_to(high[:, None, None], (heads_here, 1, HEAD_DIM)),
            jnp.broadcast_to(low[:, None, None], (heads_here, 1, HEAD_DIM)),
            jnp.zeros((heads_here, PAD_ROWS - 2, HEAD_DIM), jnp.bfloat16),
        ],
        axis=1,
    )
    packed = jnp.concatenate([local_final.astype(jnp.bfloat16), extra], axis=1)
    gathered = gather_by_exchange(packed, axis)
    finals = gathered[:, :, :HEAD_DIM, :].astype(jnp.float32)
    totals = gathered[:, :, HEAD_DIM, 0].astype(jnp.float32) + gathered[
        :, :, HEAD_DIM + 1, 0
    ].astype(jnp.float32)
    count = gathered.shape[0]
    mine = lax.axis_index(axis)
    order = jnp.arange(count, dtype=jnp.int32)
    between = (order[:, None] < order[None, :]) & (order[None, :] < mine)
    exponent = jnp.sum(jnp.where(between[:, :, None], totals[None, :, :], 0.0), axis=1)
    weight = jnp.where((order < mine)[:, None], jnp.exp(exponent), 0.0)
    return jnp.sum(weight[:, :, None, None] * finals, axis=0)


def shards(frames, log_decay, w_query, w_key, w_value, w_gate, w_out):
    head_width = w_query.shape[1]
    blocks = [w_query, w_key, w_value, w_gate, w_out]
    width = sum((block.shape[1] for block in blocks))
    column = jnp.arange(width)[None, :]
    packed = jnp.pad(blocks[-1], ((0, 0), (width - head_width, 0)))
    for start, block in reversed(list(zip(range(0, width, head_width), blocks))[:-1]):
        padded = jnp.pad(block, ((0, 0), (start, width - start - head_width)))
        packed = jnp.where(column < start + head_width, padded, packed)
    stacked = lax.all_gather(packed, "tm", axis=0, tiled=True)
    joined = stacked[:, : 4 * head_width]
    out_blocks = stacked[:, 4 * head_width :].reshape(-1, head_width, w_out.shape[1])
    frames_here = gather_by_exchange(frames, "head").reshape(-1, frames.shape[1])
    projected = jnp.dot(frames_here, joined, preferred_element_type=jnp.float32)
    local_len = projected.shape[0]
    heads_here = head_width // HEAD_DIM
    block_count = local_len // BLOCK
    query_blocks = (
        projected[:, :head_width]
        .astype(jnp.bfloat16)
        .reshape(block_count, BLOCK, heads_here, HEAD_DIM)
    )
    key_blocks = (
        projected[:, head_width : 2 * head_width]
        .astype(jnp.bfloat16)
        .reshape(block_count, BLOCK, heads_here, HEAD_DIM)
    )
    value_blocks = (
        projected[:, 2 * head_width : 3 * head_width]
        .astype(jnp.bfloat16)
        .reshape(block_count, BLOCK, heads_here, HEAD_DIM)
    )
    gate_all = projected[:, 3 * head_width :]
    running_blocks = jnp.cumsum(log_decay.reshape(block_count, BLOCK, heads_here), axis=1)
    slice_ordinal = jnp.arange(BLOCK, dtype=jnp.int32)
    causal = slice_ordinal[:, None] >= slice_ordinal[None, :]

    def local_step(carry_state, inputs):
        query_block, key_block, value_block, running = inputs
        gaps = running.T[:, :, None] - running.T[:, None, :]
        decay = jnp.exp(jnp.where(causal[None], gaps, -jnp.inf))
        scores = jnp.einsum(
            "thd,shd->hts", query_block, key_block, preferred_element_type=jnp.float32
        )
        weights = (scores * decay).astype(jnp.bfloat16)
        intra = jnp.einsum("hts,shd->thd", weights, value_block, preferred_element_type=jnp.float32)
        scaled = (
            key_block.astype(jnp.float32) * jnp.exp(running[-1][None, :] - running)[:, :, None]
        ).astype(jnp.bfloat16)
        update = jnp.einsum("shd,she->hde", scaled, value_block, preferred_element_type=jnp.float32)
        next_state = jnp.exp(running[-1])[:, None, None] * carry_state + update
        return (next_state, (intra, carry_state))

    zero_state = jnp.zeros((heads_here, HEAD_DIM, HEAD_DIM), jnp.float32)
    local_final, (intra_all, local_starts) = lax.scan(
        local_step, zero_state, (query_blocks, key_blocks, value_blocks, running_blocks)
    )
    prior = prior_state(local_final, jnp.sum(log_decay, axis=0), "tm")
    block_logs = running_blocks[:, -1, :]
    before = jnp.cumsum(block_logs, axis=0) - block_logs
    start_states = jnp.exp(before)[:, :, None, None] * prior[None] + local_starts
    lifted = query_blocks.astype(jnp.float32) * jnp.exp(running_blocks)[..., None]
    inter = jnp.einsum("cthd,chde->cthe", lifted, start_states, precision=lax.Precision.HIGHEST)
    retained = (intra_all + inter).reshape(local_len, heads_here, HEAD_DIM)
    center = jnp.mean(retained, axis=-1, keepdims=True)
    spread = jnp.mean((retained - center) ** 2, axis=-1, keepdims=True)
    normed = (retained - center) / jnp.sqrt(spread + 1e-05)
    gated = (
        (jax.nn.silu(gate_all.reshape(local_len, heads_here, HEAD_DIM)) * normed)
        .astype(jnp.bfloat16)
        .reshape(local_len, head_width)
    )
    heads = lax.axis_size("head")
    side = int(round(heads**0.5))
    me = lax.axis_index("head")
    row, col = (me // side, me % side)
    rows_mine = out_blocks
    ring_order = sorted(range(1, side), key=lambda shift: -min(shift, side - shift))
    by_owner = gated.reshape(side, side, local_len // heads, head_width)
    units = lax.axis_size("tm")
    half = rows_mine.shape[0] // 2
    parity = lax.axis_index("tm") % 2
    own_half = lax.dynamic_slice_in_dim(rows_mine, parity * half, half, axis=0)
    pieces = [lax.dynamic_index_in_dim(by_owner, col, axis=1, keepdims=False)]
    fetched = []
    for shift in ring_order:
        across = [(h, h // side * side + (h % side + shift) % side) for h in range(heads)]
        piece = lax.dynamic_index_in_dim(by_owner, (col + shift) % side, axis=1, keepdims=False)
        pieces.append(lax.ppermute(piece, "head", across))
        fetched.append(lax.ppermute(own_half, "head", across))
    fetched = jnp.stack(fetched)
    swapped = lax.ppermute(fetched, "tm", [(t, t ^ 1) for t in range(units)])
    first = jnp.where(parity == 0, fetched, swapped)
    second = jnp.where(parity == 0, swapped, fetched)
    remote = jnp.concatenate([first, second], axis=1)
    weights_in = [rows_mine] + [remote[s] for s in range(side - 1)]
    partial = jnp.einsum(
        "syfr,skrc->yfkc",
        jnp.stack(pieces),
        jnp.stack(weights_in),
        preferred_element_type=jnp.float32,
    ).astype(jnp.bfloat16)
    partial = partial.reshape(side, local_len // heads, -1)
    total = lax.dynamic_index_in_dim(partial, row, axis=0, keepdims=False).astype(jnp.float32)
    for shift in ring_order:
        down = [(h, (h // side + shift) % side * side + h % side) for h in range(heads)]
        piece = lax.dynamic_index_in_dim(partial, (row + shift) % side, axis=0, keepdims=False)
        total = total + lax.ppermute(piece, "head", down).astype(jnp.float32)
    return total.astype(jnp.bfloat16)


def solution(mesh):
    return jax.shard_map(
        shards,
        mesh=mesh,
        in_specs=(
            P(("tm", "head"), None),
            P("tm", "head"),
            P("tm", "head"),
            P("tm", "head"),
            P("tm", "head"),
            P("tm", "head"),
            P("head", "tm"),
        ),
        out_specs=P(("tm", "head"), None),
        check_vma=False,
    )
```

profile of v0, /device:TPU:6, one launch (start us, length us, event | category | flops | bytes accessed | tf_op | source)
XLA Modules:
  0.0 110.7 jit_solution(12447846987612990103)
XLA Ops:
  6.5 0.0 all-gather.2.cloned.1.call-start
  6.5 1.6 %select_select_fusion = bf16[128,640]{1,0:T(8,128)(2,1)} fusion(bf16[128,128]{1,0:T(8,128)(2,1)} %param.13, bf16[128,128]{1,0:T(8,128)(2,1)} %param.12, bf16[128,128]{1,0:T(8,128)(2,1)} %param.11, bf16[128,128]{1,0:T(8,128)(2,1)} %param.10, bf16[128,128]{1,0:T(8,128)(2,1)} %param.9, pred[640]{0:T(1024)(128)(4,1)S(1)} %get-tuple-element.47, ...), kind=kLoop, calls=%fused_computation.47 | loop fusion | flops 327680 | bytes 330240 | tf_op jit(solution)/shard_map/jit(_where)/select_n | solution.py:52
  8.1 0.0 all-gather.2.cloned.1.call-update
  8.1 2.5 %broadcast_in_dim.113 = bf16[16,32,2048]{2,1,0:T(8,128)(2,1)} broadcast(bf16[32,2048]{1,0:T(8,128)(2,1)} %param.7), dimensions={1,2} | broadcast | bytes 2228224 | tf_op jit(solution)/shard_map/broadcast_in_dim | solution.py:13
  10.6 0.0 copy-start.1
  10.6 7.6 %all-to-all-start = ((bf16[16,32,2048]{2,1,0:T(8,128)(2,1)}), bf16[16,32,2048]{2,1,0:T(8,128)(2,1)S(1)}, u32[]{:S(2)}, u32[]{:S(2)}) async-start(bf16[16,32,2048]{2,1,0:T(8,128)(2,1)} %broadcast_in_dim.113), calls=%async_computation | async-start | bytes 4194304 | tf_op jit(solution)/shard_map/all_to_all | solution.py:14
  18.2 0.0 copy-done.1
  18.2 0.7 reduce_sum.47
  18.8 0.3 reduce-window.6
  19.1 0.2 slice_reduce_fusion
  19.3 0.2 reduce-window.9
  19.5 0.1 broadcast.193
  19.6 0.6 slice.69
  20.1 0.6 slice.68
  23.3 0.1 pad.37.clone
  23.4 0.1 pad.38.clone
  23.5 0.1 subtract_exponential_fusion
  23.6 22.9 %all-to-all-done = bf16[16,32,2048]{2,1,0:T(8,128)(2,1)S(1)} async-done(((bf16[16,32,2048]{2,1,0:T(8,128)(2,1)}), bf16[16,32,2048]{2,1,0:T(8,128)(2,1)S(1)}, u32[]{:S(2)}, u32[]{:S(2)}) %all-to-all-start) | async-done | bytes 2097184 | tf_op jit(solution)/shard_map/all_to_all | solution.py:14
  46.4 6.1 %all-gather.2.cloned.1.call-done = bf16[2048,640]{1,0:T(8,128)(2,1)} async-done(((bf16[128,640]{1,0:T(8,128)(2,1)}), bf16[2048,640]{1,0:T(8,128)(2,1)}) %all-gather.2.cloned.1.call-update) | async-done | bytes 2621456 | tf_op jit(solution)/shard_map/all_gather | solution.py:53
  52.6 3.8 %fusion.58 = (bf16[512,512]{1,0:T(8,128)(2,1)S(1)}, f32[512,512]{1,0:T(8,128)}) fusion(bf16[512,2048]{1,0:T(8,128)(2,1)S(1)} %bitcast.110, bf16[2048,640]{1,0:T(8,128)(2,1)} %all-gather.2.cloned.1.call-done), kind=kOutput, calls=%fused_computation.95 | convolution fusion | flops 1074003968 | bytes 5767168 | tf_op jit(solution)/shard_map/dot_general | solution.py:57
  56.4 0.0 copy-start
  56.4 0.3 fusion.18
  56.8 0.1 maximum_bitcast_fusion.10
  56.9 0.9 broadcast_in_dim.122
  57.8 4.0 %all-to-all-start.1 = ((bf16[16,1,136,128]{3,2,1,0:T(8,128)(2,1)}), bf16[16,1,136,128]{3,2,1,0:T(8,128)(2,1)S(1)}, u32[]{:S(2)}, u32[]{:S(2)}) async-start(bf16[16,1,136,128]{3,2,1,0:T(8,128)(2,1)} %broadcast_in_dim.122), calls=%async_computation.1 | async-start | bytes 1114112 | tf_op jit(solution)/shard_map/all_to_all | solution.py:14
  62.0 0.6 slice.67
  62.6 0.6 slice.66
  64.4 1.1 slice.73
  65.6 1.5 %collective-permute-start.3 = (bf16[8,128,128]{2,1,0:T(8,128)(2,1)S(1)}, bf16[8,128,128]{2,1,0:T(8,128)(2,1)S(1)}, u32[]{:S(2)}, u32[]{:S(2)}) collective-permute-start(bf16[8,128,128]{2,1,0:T(8,128)(2,1)S(1)} %constant_dynamic-slice_fusion), channel_id=1, source_target_pairs={{0,2},{1,3},{2,0},{3,1},{4,6},{5,7},{6,4},{7,5},{8,10},{9,11},{10,... | collective-permute-start | bytes 786440 | tf_op jit(solution)/shard_map/ppermute | solution.py:133
  67.1 2.4 %collective-permute-start.4 = (bf16[8,128,128]{2,1,0:T(8,128)(2,1)S(1)}, bf16[8,128,128]{2,1,0:T(8,128)(2,1)S(1)}, u32[]{:S(2)}, u32[]{:S(2)}) collective-permute-start(bf16[8,128,128]{2,1,0:T(8,128)(2,1)S(1)} %constant_dynamic-slice_fusion), channel_id=1, source_target_pairs={{0,1},{1,2},{2,3},{3,0},{4,5},{5,6},{6,7},{7,4},{8,9},{9,10},{10,1... | collective-permute-start | bytes 786440 | tf_op jit(solution)/shard_map/ppermute | solution.py:133
  69.5 0.0 collective-permute-start.5
  69.5 1.2 %fusion.15 = f32[1,512,1,128]{3,1,2,0:T(8,128)} fusion(f32[512]{0:T(512)S(1)} %get-tuple-element.22, bf16[512,512]{1,0:T(8,128)(2,1)S(1)} %get-tuple-element.43), kind=kOutput, calls=%fused_computation.16 | convolution fusion | flops 135528448 | bytes 659456 | tf_op jit(solution)/shard_map/while/body/eval_jaxpr/hts,shd->thd/dot_general | solution.py:89
  70.7 0.0 copy-done
  70.7 5.6 %collective-permute-done.3 = bf16[8,128,128]{2,1,0:T(8,128)(2,1)S(1)} collective-permute-done((bf16[8,128,128]{2,1,0:T(8,128)(2,1)S(1)}, bf16[8,128,128]{2,1,0:T(8,128)(2,1)S(1)}, u32[]{:S(2)}, u32[]{:S(2)}) %collective-permute-start.3) | collective-permute-done | bytes 262176 | tf_op jit(solution)/shard_map/ppermute | solution.py:133
  76.3 4.1 %collective-permute-done.4 = bf16[8,128,128]{2,1,0:T(8,128)(2,1)S(1)} collective-permute-done((bf16[8,128,128]{2,1,0:T(8,128)(2,1)S(1)}, bf16[8,128,128]{2,1,0:T(8,128)(2,1)S(1)}, u32[]{:S(2)}, u32[]{:S(2)}) %collective-permute-start.4) | collective-permute-done | bytes 262176 | tf_op jit(solution)/shard_map/ppermute | solution.py:133
  80.5 0.8 collective-permute-done.5
  81.3 0.1 pad_maximum_fusion
  81.3 0.1 collective-permute-start.6
  81.4 0.0 all-to-all-done.1
  81.5 0.2 fusion.55
  81.7 0.1 select_reduce_fusion
  81.8 0.2 multiply_reduce_fusion
  82.0 1.5 %fusion.59 = (f32[512]{0:T(512)S(1)}, f32[1,512,1,128]{3,1,2,0:T(8,128)S(1)}) fusion(f32[1,512,1,128]{3,1,2,0:T(8,128)} %fusion.15, f32[512]{0:T(512)S(1)} %exp.53, bf16[512,512]{1,0:T(8,128)(2,1)} %copy-done, f32[128,128]{1,0:T(8,128)S(1)} %multiply_reduce_fusion, f32[]{:T(128)} %bitcast.11), kind=kOutput, calls=%fused_computation.96 | convolution fusion | flops 100941312 | bytes 725504 | tf_op jit(solution)/shard_map/cthd,chde->cthe/dot_general | solution.py:106
  83.5 0.2 fusion.29
  83.8 1.2 %fusion.32 = bf16[512,128]{1,0:T(8,128)(2,1)S(1)} fusion(f32[1,512,1,128]{3,1,2,0:T(8,128)S(1)} %get-tuple-element.46, f32[512,512]{1,0:T(8,128)} %get-tuple-element.44, f32[512]{0:T(512)S(1)} %add_sqrt_fusion, f32[512]{0:T(512)S(1)} %broadcast_multiply_fusion), kind=kLoop, calls=%fused_computation.43 | loop fusion | flops 524288 | bytes 659456 | tf_op jit(solution)/shard_map/convert_element_type | solution.py:113
  85.0 1.9 %collective-permute-start = (bf16[4,32,128]{2,1,0:T(8,128)(2,1)S(1)}, bf16[4,32,128]{2,1,0:T(8,128)(2,1)S(1)}, u32[]{:S(2)}, u32[]{:S(2)}) collective-permute-start(bf16[4,32,128]{2,1,0:T(8,128)(2,1)S(1)} %get-tuple-element.42), channel_id=1, source_target_pairs={{0,2},{1,3},{2,0},{3,1},{4,6},{5,7},{6,4},{7,5},{8,10},{9,11},{10,... | collective-permute-start | bytes 98312 | tf_op jit(solution)/shard_map/ppermute | solution.py:132
  86.9 1.8 %collective-permute-start.1 = (bf16[4,32,128]{2,1,0:T(8,128)(2,1)S(1)}, bf16[4,32,128]{2,1,0:T(8,128)(2,1)S(1)}, u32[]{:S(2)}, u32[]{:S(2)}) collective-permute-start(bf16[4,32,128]{2,1,0:T(8,128)(2,1)S(1)} %get-tuple-element.41), channel_id=1, source_target_pairs={{0,1},{1,2},{2,3},{3,0},{4,5},{5,6},{6,7},{7,4},{8,9},{9,10},{10,1... | collective-permute-start | bytes 98312 | tf_op jit(solution)/shard_map/ppermute | solution.py:132
  88.7 0.2 collective-permute-start.2
  88.9 0.0 collective-permute-done.6
  88.9 0.1 broadcast_select_fusion.1
  89.0 1.5 %collective-permute-done = bf16[4,32,128]{2,1,0:T(8,128)(2,1)S(1)} collective-permute-done((bf16[4,32,128]{2,1,0:T(8,128)(2,1)S(1)}, bf16[4,32,128]{2,1,0:T(8,128)(2,1)S(1)}, u32[]{:S(2)}, u32[]{:S(2)}) %collective-permute-start) | collective-permute-done | bytes 32800 | tf_op jit(solution)/shard_map/ppermute | solution.py:132
  90.5 0.3 collective-permute-done.1
  90.8 3.0 %collective-permute-done.2 = bf16[4,32,128]{2,1,0:T(8,128)(2,1)S(1)} collective-permute-done((bf16[4,32,128]{2,1,0:T(8,128)(2,1)S(1)}, bf16[4,32,128]{2,1,0:T(8,128)(2,1)S(1)}, u32[]{:S(2)}, u32[]{:S(2)}) %collective-permute-start.2) | collective-permute-done | bytes 32800 | tf_op jit(solution)/shard_map/ppermute | solution.py:132
  93.8 0.5 fusion.13
  94.2 0.1 copy.38
  94.4 2.2 %collective-permute-start.7 = (bf16[32,2048]{1,0:T(8,128)(2,1)S(1)}, bf16[32,2048]{1,0:T(8,128)(2,1)S(1)}, u32[]{:S(2)}, u32[]{:S(2)}) collective-permute-start(bf16[32,2048]{1,0:T(8,128)(2,1)S(1)} %get-tuple-element.25), channel_id=1, source_target_pairs={{0,8},{1,9},{2,10},{3,11},{4,12},{5,13},{6,14},{7,15},{8,0},{9,1},... | collective-permute-start | bytes 393224 | tf_op jit(solution)/shard_map/ppermute | solution.py:151
  96.6 0.6 collective-permute-start.8
  97.2 2.6 %collective-permute-start.9 = (bf16[32,2048]{1,0:T(8,128)(2,1)S(1)}, bf16[32,2048]{1,0:T(8,128)(2,1)S(1)}, u32[]{:S(2)}, u32[]{:S(2)}) collective-permute-start(bf16[32,2048]{1,0:T(8,128)(2,1)S(1)} %get-tuple-element.26), channel_id=1, source_target_pairs={{0,12},{1,13},{2,14},{3,15},{4,0},{5,1},{6,2},{7,3},{8,4},{9,5},{1... | collective-permute-start | bytes 393224 | tf_op jit(solution)/shard_map/ppermute | solution.py:151
  99.8 1.9 %collective-permute-done.7 = bf16[32,2048]{1,0:T(8,128)(2,1)S(1)} collective-permute-done((bf16[32,2048]{1,0:T(8,128)(2,1)S(1)}, bf16[32,2048]{1,0:T(8,128)(2,1)S(1)}, u32[]{:S(2)}, u32[]{:S(2)}) %collective-permute-start.7) | collective-permute-done | bytes 131104 | tf_op jit(solution)/shard_map/ppermute | solution.py:151
  101.7 1.4 %collective-permute-done.8 = bf16[32,2048]{1,0:T(8,128)(2,1)S(1)} collective-permute-done((bf16[32,2048]{1,0:T(8,128)(2,1)S(1)}, bf16[32,2048]{1,0:T(8,128)(2,1)S(1)}, u32[]{:S(2)}, u32[]{:S(2)}) %collective-permute-start.8) | collective-permute-done | bytes 131104 | tf_op jit(solution)/shard_map/ppermute | solution.py:151
  103.1 0.0 collective-permute-done.9
  103.1 0.7 fusion.27
  (13 shorter events, 0.1 us)
Async XLA Ops:
  6.5 46.1 %all-gather.2.cloned.1.call-start = ((), (), s32[]{:S(2)}) async-start(), calls=%async_computation.2 | async-start | bytes 2785280 | tf_op jit(solution)/shard_map/all_gather | solution.py:53
  10.6 7.6 %copy-start.1 = (f32[512,1]{0,1:T(1,128)S(1)}, f32[512,1]{0,1:T(1,128)}, u32[]{:S(2)}) copy-start(f32[512,1]{0,1:T(1,128)} %param.8) | copy-start | bytes 6148
  10.6 35.8 %all-to-all-start = ((bf16[16,32,2048]{2,1,0:T(8,128)(2,1)}), bf16[16,32,2048]{2,1,0:T(8,128)(2,1)S(1)}, u32[]{:S(2)}, u32[]{:S(2)}) async-start(bf16[16,32,2048]{2,1,0:T(8,128)(2,1)} %broadcast_in_dim.113), calls=%async_computation | async-start | bytes 4194304 | tf_op jit(solution)/shard_map/all_to_all | solution.py:14
  56.4 14.3 %copy-start = (bf16[512,512]{1,0:T(8,128)(2,1)}, bf16[512,512]{1,0:T(8,128)(2,1)S(1)}, u32[]{:S(2)}) copy-start(bf16[512,512]{1,0:T(8,128)(2,1)S(1)} %get-tuple-element.43) | copy-start | bytes 1572868
  57.8 23.7 %all-to-all-start.1 = ((bf16[16,1,136,128]{3,2,1,0:T(8,128)(2,1)}), bf16[16,1,136,128]{3,2,1,0:T(8,128)(2,1)S(1)}, u32[]{:S(2)}, u32[]{:S(2)}) async-start(bf16[16,1,136,128]{3,2,1,0:T(8,128)(2,1)} %broadcast_in_dim.122), calls=%async_computation.1 | async-start | bytes 1114112 | tf_op jit(solution)/shard_map/all_to_all | solution.py:14
  65.6 10.8 %collective-permute-start.3 = (bf16[8,128,128]{2,1,0:T(8,128)(2,1)S(1)}, bf16[8,128,128]{2,1,0:T(8,128)(2,1)S(1)}, u32[]{:S(2)}, u32[]{:S(2)}) collective-permute-start(bf16[8,128,128]{2,1,0:T(8,128)(2,1)S(1)} %constant_dynamic-slice_fusion), channel_id=1, source_target_pairs={{0,2},{1,3},{2,0},{3,1},{4,6},{5,7},{6,4},{7,5},{8,10},{9,11},{10,... | collective-permute-start | bytes 786440 | tf_op jit(solution)/shard_map/ppermute | solution.py:133
  67.1 13.4 %collective-permute-start.4 = (bf16[8,128,128]{2,1,0:T(8,128)(2,1)S(1)}, bf16[8,128,128]{2,1,0:T(8,128)(2,1)S(1)}, u32[]{:S(2)}, u32[]{:S(2)}) collective-permute-start(bf16[8,128,128]{2,1,0:T(8,128)(2,1)S(1)} %constant_dynamic-slice_fusion), channel_id=1, source_target_pairs={{0,1},{1,2},{2,3},{3,0},{4,5},{5,6},{6,7},{7,4},{8,9},{9,10},{10,1... | collective-permute-start | bytes 786440 | tf_op jit(solution)/shard_map/ppermute | solution.py:133
  69.5 11.8 %collective-permute-start.5 = (bf16[8,128,128]{2,1,0:T(8,128)(2,1)S(1)}, bf16[8,128,128]{2,1,0:T(8,128)(2,1)S(1)}, u32[]{:S(2)}, u32[]{:S(2)}) collective-permute-start(bf16[8,128,128]{2,1,0:T(8,128)(2,1)S(1)} %constant_dynamic-slice_fusion), channel_id=1, source_target_pairs={{0,3},{1,0},{2,1},{3,2},{4,7},{5,4},{6,5},{7,6},{8,11},{9,8},{10,9... | collective-permute-start | bytes 786440 | tf_op jit(solution)/shard_map/ppermute | solution.py:133
  81.3 7.5 %collective-permute-start.6 = (bf16[3,8,128,128]{3,2,0,1:T(8,128)(2,1)S(1)}, bf16[3,8,128,128]{3,2,0,1:T(8,128)(2,1)S(1)}, u32[]{:S(2)}, u32[]{:S(2)}) collective-permute-start(bf16[3,8,128,128]{3,2,0,1:T(8,128)(2,1)S(1)} %pad_maximum_fusion), channel_id=1, source_target_pairs={{0,16},{16,0},{32,48},{48,32},{64,80},{80,64},{96,112},{112,96},{1... | collective-permute-start | bytes 2359304 | tf_op jit(solution)/shard_map/ppermute | solution.py:135
  85.0 5.5 %collective-permute-start = (bf16[4,32,128]{2,1,0:T(8,128)(2,1)S(1)}, bf16[4,32,128]{2,1,0:T(8,128)(2,1)S(1)}, u32[]{:S(2)}, u32[]{:S(2)}) collective-permute-start(bf16[4,32,128]{2,1,0:T(8,128)(2,1)S(1)} %get-tuple-element.42), channel_id=1, source_target_pairs={{0,2},{1,3},{2,0},{3,1},{4,6},{5,7},{6,4},{7,5},{8,10},{9,11},{10,... | collective-permute-start | bytes 98312 | tf_op jit(solution)/shard_map/ppermute | solution.py:132
  86.9 3.9 %collective-permute-start.1 = (bf16[4,32,128]{2,1,0:T(8,128)(2,1)S(1)}, bf16[4,32,128]{2,1,0:T(8,128)(2,1)S(1)}, u32[]{:S(2)}, u32[]{:S(2)}) collective-permute-start(bf16[4,32,128]{2,1,0:T(8,128)(2,1)S(1)} %get-tuple-element.41), channel_id=1, source_target_pairs={{0,1},{1,2},{2,3},{3,0},{4,5},{5,6},{6,7},{7,4},{8,9},{9,10},{10,1... | collective-permute-start | bytes 98312 | tf_op jit(solution)/shard_map/ppermute | solution.py:132
  88.7 5.1 %collective-permute-start.2 = (bf16[4,32,128]{2,1,0:T(8,128)(2,1)S(1)}, bf16[4,32,128]{2,1,0:T(8,128)(2,1)S(1)}, u32[]{:S(2)}, u32[]{:S(2)}) collective-permute-start(bf16[4,32,128]{2,1,0:T(8,128)(2,1)S(1)} %get-tuple-element.40), channel_id=1, source_target_pairs={{0,3},{1,0},{2,1},{3,2},{4,7},{5,4},{6,5},{7,6},{8,11},{9,8},{10,9... | collective-permute-start | bytes 98312 | tf_op jit(solution)/shard_map/ppermute | solution.py:132
  94.4 7.3 %collective-permute-start.7 = (bf16[32,2048]{1,0:T(8,128)(2,1)S(1)}, bf16[32,2048]{1,0:T(8,128)(2,1)S(1)}, u32[]{:S(2)}, u32[]{:S(2)}) collective-permute-start(bf16[32,2048]{1,0:T(8,128)(2,1)S(1)} %get-tuple-element.25), channel_id=1, source_target_pairs={{0,8},{1,9},{2,10},{3,11},{4,12},{5,13},{6,14},{7,15},{8,0},{9,1},... | collective-permute-start | bytes 393224 | tf_op jit(solution)/shard_map/ppermute | solution.py:151
  96.6 6.5 %collective-permute-start.8 = (bf16[32,2048]{1,0:T(8,128)(2,1)S(1)}, bf16[32,2048]{1,0:T(8,128)(2,1)S(1)}, u32[]{:S(2)}, u32[]{:S(2)}) collective-permute-start(bf16[32,2048]{1,0:T(8,128)(2,1)S(1)} %get-tuple-element.36), channel_id=1, source_target_pairs={{0,4},{1,5},{2,6},{3,7},{4,8},{5,9},{6,10},{7,11},{8,12},{9,13},{1... | collective-permute-start | bytes 393224 | tf_op jit(solution)/shard_map/ppermute | solution.py:151
  97.2 5.9 %collective-permute-start.9 = (bf16[32,2048]{1,0:T(8,128)(2,1)S(1)}, bf16[32,2048]{1,0:T(8,128)(2,1)S(1)}, u32[]{:S(2)}, u32[]{:S(2)}) collective-permute-start(bf16[32,2048]{1,0:T(8,128)(2,1)S(1)} %get-tuple-element.26), channel_id=1, source_target_pairs={{0,12},{1,13},{2,14},{3,15},{4,0},{5,1},{6,2},{7,3},{8,4},{9,5},{1... | collective-permute-start | bytes 393224 | tf_op jit(solution)/shard_map/ppermute | solution.py:151
Sparse Core Ops, SparseCore 0:
  9.2 43.3 all-gather.1
where the time goes:
time: 111 us
  waiting for transfers between devices  47.6 us (43%)
  starting transfers between devices  24.9 us (22%)
  between operations  17.6 us (16%)
  matrix products  7.4 us (7%)
  local copies, waits for them, and re-layouts  7.38 us (7%)
  other arithmetic  5.77 us (5%)
    all_to_all x2, waiting for transfers between devices, gather_by_exchange(): return lax.all_to_all(copies, axis, 0, 0, tiled=False)  22.9 us
    all_to_all x2, starting transfers between devices, gather_by_exchange(): return lax.all_to_all(copies, axis, 0, 0, tiled=False)  11.6 us
    ppermute x3, waiting for transfers between devices, shards(): fetched.append(lax.ppermute(own_half, 'head', across))  10.5 us
    all_gather x1, waiting for transfers between devices, shards(): stacked = lax.all_gather(packed, 'tm', axis=0, tiled=True)  6.14 us
    ppermute x3, starting transfers between devices, shards(): total = total + lax.ppermute(piece, 'head', down).astype(jnp.float32)  5.39 us
    ppermute x3, waiting for transfers between devices, shards(): pieces.append(lax.ppermute(piece, 'head', across))  4.76 us
    ppermute x3, starting transfers between devices, shards(): pieces.append(lax.ppermute(piece, 'head', across))  3.92 us
    ppermute x3, starting transfers between devices, shards(): fetched.append(lax.ppermute(own_half, 'head', across))  3.91 us
  transfers between devices with their start and end apart: 13, of which 10 were waited for; matrix products, arithmetic and copies ran while one was open for 11% of the time, Pallas kernels for 0%

commit v1 on v0

--- a/solution.py
+++ b/solution.py
@@ -6,6 +6,28 @@
 HEAD_DIM = 128
 BLOCK = 512
 PAD_ROWS = 8
+
+
+def in_order(pieces, dim):
+    pieces = jnp.moveaxis(pieces, 0, dim)
+    dims = pieces.shape
+    return pieces.reshape(*dims[:dim], dims[dim] * dims[dim + 1], *dims[dim + 2 :])
+
+
+def collect(shard, axis, dim):
+    size = lax.axis_size(axis)
+    pairs = [(i, (i + 1) % size) for i in range(size)]
+    back = [(b, a) for a, b in pairs]
+    lower, upper = ([], [])
+    for hop in range(size - 1):
+        if hop % 2 == 0:
+            lower.append(lax.ppermute(lower[-1] if lower else shard, axis, pairs))
+        else:
+            upper.append(lax.ppermute(upper[-1] if upper else shard, axis, back))
+    parts = jnp.stack([*lower[::-1], shard, *upper])
+    shift = lax.axis_index(axis) - len(lower)
+    parts = parts[(jnp.arange(size) - shift) % size]
+    return in_order(parts, dim)
 
 
 def gather_by_exchange(part, axis):
@@ -50,7 +72,7 @@
     for start, block in reversed(list(zip(range(0, width, head_width), blocks))[:-1]):
         padded = jnp.pad(block, ((0, 0), (start, width - start - head_width)))
         packed = jnp.where(column < start + head_width, padded, packed)
-    stacked = lax.all_gather(packed, "tm", axis=0, tiled=True)
+    stacked = collect(packed, "tm", 0)
     joined = stacked[:, : 4 * head_width]
     out_blocks = stacked[:, 4 * head_width :].reshape(-1, head_width, w_out.shape[1])
     frames_here = gather_by_exchange(frames, "head").reshape(-1, frames.shape[1])

time: 111 us -> 126 us (1.14)
  starting transfers between devices: 24.9 us -> 49.3 us
  local copies, waits for them, and re-layouts: 7.38 us -> 21.7 us
  between operations: 17.6 us -> 4.17 us
  waiting for transfers between devices: 47.6 us -> 37.9 us
    all_to_all x2, waiting for transfers between devices: 22.9 us -> 0.01 us  [gather_by_exchange(): return lax.all_to_all(copies, axis, 0, 0, tiled=False)]
    ppermute x0 -> x15, starting transfers between devices: none -> 21.8 us  [the longest x7 21.8 us: collect(): upper.append(lax.ppermute(upper[-1] if upper else shard, axis, back))]
    ppermute x0 -> x15, waiting for transfers between devices: none -> 21 us  [the longest x8 17.3 us: collect(): lower.append(lax.ppermute(lower[-1] if lower else shard, axis, pairs))]
    unnamed x4 -> x23, local copies, waits for them, and re-layouts: 0.01 us -> 11.8 us
    all_gather x1 -> x0, waiting for transfers between devices: 6.14 us -> none  [shards(): stacked = lax.all_gather(packed, 'tm', axis=0, tiled=True)]
    gather x0 -> x1, local copies, waits for them, and re-layouts: none -> 2.76 us  [collect(): parts = parts[(jnp.arange(size) - shift) % size]]
    all_to_all x2, starting transfers between devices: 11.6 us -> 13.8 us  [gather_by_exchange(): return lax.all_to_all(copies, axis, 0, 0, tiled=False)]
  transfers between devices with their start and end apart: 13 -> 27, of which waited for: 10 -> 14; matrix products, arithmetic and copies ran while one was open for 11% -> 20% of each run, Pallas kernels for 0% -> 0%
where the time goes in v1:
time: 126 us
  starting transfers between devices  49.3 us (39%)
  waiting for transfers between devices  37.9 us (30%)
  local copies, waits for them, and re-layouts  21.7 us (17%)
  matrix products  7.66 us (6%)
  other arithmetic  5.06 us (4%)
  between operations  4.17 us (3%)
    ppermute x7, starting transfers between devices, collect(): upper.append(lax.ppermute(upper[-1] if upper else shard, axis, back))  21.8 us
    ppermute x8, waiting for transfers between devices, collect(): lower.append(lax.ppermute(lower[-1] if lower else shard, axis, pairs))  17.3 us
    all_to_all x2, starting transfers between devices, gather_by_exchange(): return lax.all_to_all(copies, axis, 0, 0, tiled=False)  13.8 us
    unnamed x23, local copies, waits for them, and re-layouts  11.8 us
    ppermute x3, waiting for transfers between devices, shards(): fetched.append(lax.ppermute(own_half, 'head', across))  9.69 us
    ppermute x3, starting transfers between devices, shards(): total = total + lax.ppermute(piece, 'head', down).astype(jnp.float32)  6.29 us
    ppermute x3, waiting for transfers between devices, shards(): pieces.append(lax.ppermute(piece, 'head', across))  4.09 us
    dot_general x1, matrix products, shards(): projected = jnp.dot(frames_here, joined, preferred_element_type=jnp.float32)  3.82 us
  transfers between devices with their start and end apart: 27, of which 14 were waited for; matrix products, arithmetic and copies ran while one was open for 20% of the time, Pallas kernels for 0%

profile of v1, /device:TPU:6, one launch (start us, length us, event | category | flops | bytes accessed | tf_op | source)
XLA Modules:
  0.0 125.8 jit_solution(15182297479111206710)
XLA Ops:
  0.0 0.9 select_select_fusion
  0.9 8.3 %collective-permute-done = bf16[128,640]{1,0:T(8,128)(2,1)S(1)} collective-permute-done((bf16[128,640]{1,0:T(8,128)(2,1)S(1)}, bf16[128,640]{1,0:T(8,128)(2,1)S(1)}, u32[]{:S(2)}, u32[]{:S(2)}) %collective-permute-start) | collective-permute-done | bytes 163872 | tf_op jit(solution)/shard_map/ppermute | solution.py:24
  9.2 3.0 %collective-permute-start.8 = (bf16[128,640]{1,0:T(8,128)(2,1)S(1)}, bf16[128,640]{1,0:T(8,128)(2,1)S(1)}, u32[]{:S(2)}, u32[]{:S(2)}) collective-permute-start(bf16[128,640]{1,0:T(8,128)(2,1)S(1)} %select_select_fusion), channel_id=1, source_target_pairs={{16,0},{32,16},{48,32},{64,48},{80,64},{96,80},{112,96},{128,112},... | collective-permute-start | bytes 491528 | tf_op jit(solution)/shard_map/ppermute | solution.py:26
  12.2 3.0 %collective-permute-done.1 = bf16[128,640]{1,0:T(8,128)(2,1)S(1)} collective-permute-done((bf16[128,640]{1,0:T(8,128)(2,1)S(1)}, bf16[128,640]{1,0:T(8,128)(2,1)S(1)}, u32[]{:S(2)}, u32[]{:S(2)}) %collective-permute-start.1) | collective-permute-done | bytes 163872 | tf_op jit(solution)/shard_map/ppermute | solution.py:24
  15.2 3.0 %collective-permute-start.9 = (bf16[128,640]{1,0:T(8,128)(2,1)S(1)}, bf16[128,640]{1,0:T(8,128)(2,1)S(1)}, u32[]{:S(2)}, u32[]{:S(2)}) collective-permute-start(bf16[128,640]{1,0:T(8,128)(2,1)S(1)} %collective-permute-done.8), channel_id=1, source_target_pairs={{16,0},{32,16},{48,32},{64,48},{80,64},{96,80},{112,96},{128,112},... | collective-permute-start | bytes 491528 | tf_op jit(solution)/shard_map/ppermute | solution.py:26
  18.1 3.0 %collective-permute-done.2 = bf16[128,640]{1,0:T(8,128)(2,1)S(1)} collective-permute-done((bf16[128,640]{1,0:T(8,128)(2,1)S(1)}, bf16[128,640]{1,0:T(8,128)(2,1)S(1)}, u32[]{:S(2)}, u32[]{:S(2)}) %collective-permute-start.2) | collective-permute-done | bytes 163872 | tf_op jit(solution)/shard_map/ppermute | solution.py:24
  21.1 3.0 %collective-permute-start.10 = (bf16[128,640]{1,0:T(8,128)(2,1)S(1)}, bf16[128,640]{1,0:T(8,128)(2,1)S(1)}, u32[]{:S(2)}, u32[]{:S(2)}) collective-permute-start(bf16[128,640]{1,0:T(8,128)(2,1)S(1)} %collective-permute-done.9), channel_id=1, source_target_pairs={{16,0},{32,16},{48,32},{64,48},{80,64},{96,80},{112,96},{128,112},... | collective-permute-start | bytes 491528 | tf_op jit(solution)/shard_map/ppermute | solution.py:26
  24.1 3.0 %collective-permute-done.3 = bf16[128,640]{1,0:T(8,128)(2,1)S(1)} collective-permute-done((bf16[128,640]{1,0:T(8,128)(2,1)S(1)}, bf16[128,640]{1,0:T(8,128)(2,1)S(1)}, u32[]{:S(2)}, u32[]{:S(2)}) %collective-permute-start.3) | collective-permute-done | bytes 163872 | tf_op jit(solution)/shard_map/ppermute | solution.py:24
  27.1 2.5 %broadcast_in_dim.114 = bf16[16,32,2048]{2,1,0:T(8,128)(2,1)} broadcast(bf16[32,2048]{1,0:T(8,128)(2,1)} %param.7), dimensions={1,2} | broadcast | bytes 2228224 | tf_op jit(solution)/shard_map/broadcast_in_dim | solution.py:35
  29.6 7.6 %all-to-all-start = ((bf16[16,32,2048]{2,1,0:T(8,128)(2,1)}), bf16[16,32,2048]{2,1,0:T(8,128)(2,1)}, u32[]{:S(2)}, u32[]{:S(2)}) async-start(bf16[16,32,2048]{2,1,0:T(8,128)(2,1)} %broadcast_in_dim.114), calls=%async_computation | async-start | bytes 4194304 | tf_op jit(solution)/shard_map/all_to_all | solution.py:36
  37.9 2.4 %collective-permute-start.11 = (bf16[128,640]{1,0:T(8,128)(2,1)S(1)}, bf16[128,640]{1,0:T(8,128)(2,1)S(1)}, u32[]{:S(2)}, u32[]{:S(2)}) collective-permute-start(bf16[128,640]{1,0:T(8,128)(2,1)S(1)} %collective-permute-done.10), channel_id=1, source_target_pairs={{16,0},{32,16},{48,32},{64,48},{80,64},{96,80},{112,96},{128,112},... | collective-permute-start | bytes 491528 | tf_op jit(solution)/shard_map/ppermute | solution.py:26
  40.3 0.6 slice.71
  40.9 0.6 slice.70
  43.1 3.5 %collective-permute-start.12 = (bf16[128,640]{1,0:T(8,128)(2,1)S(1)}, bf16[128,640]{1,0:T(8,128)(2,1)S(1)}, u32[]{:S(2)}, u32[]{:S(2)}) collective-permute-start(bf16[128,640]{1,0:T(8,128)(2,1)S(1)} %collective-permute-done.11), channel_id=1, source_target_pairs={{16,0},{32,16},{48,32},{64,48},{80,64},{96,80},{112,96},{128,112},... | collective-permute-start | bytes 491528 | tf_op jit(solution)/shard_map/ppermute | solution.py:26
  46.7 2.8 %collective-permute-done.12 = bf16[128,640]{1,0:T(8,128)(2,1)S(1)} collective-permute-done((bf16[128,640]{1,0:T(8,128)(2,1)S(1)}, bf16[128,640]{1,0:T(8,128)(2,1)S(1)}, u32[]{:S(2)}, u32[]{:S(2)}) %collective-permute-start.12) | collective-permute-done | bytes 163872 | tf_op jit(solution)/shard_map/ppermute | solution.py:26
  49.4 3.5 %collective-permute-start.13 = (bf16[128,640]{1,0:T(8,128)(2,1)S(1)}, bf16[128,640]{1,0:T(8,128)(2,1)S(1)}, u32[]{:S(2)}, u32[]{:S(2)}) collective-permute-start(bf16[128,640]{1,0:T(8,128)(2,1)S(1)} %collective-permute-done.12), channel_id=1, source_target_pairs={{16,0},{32,16},{48,32},{64,48},{80,64},{96,80},{112,96},{128,112},... | collective-permute-start | bytes 491528 | tf_op jit(solution)/shard_map/ppermute | solution.py:26
  53.0 0.6 reduce_sum.47
  55.1 0.7 collective-permute-done.13
  55.8 3.5 %collective-permute-start.14 = (bf16[128,640]{1,0:T(8,128)(2,1)S(1)}, bf16[128,640]{1,0:T(8,128)(2,1)S(1)}, u32[]{:S(2)}, u32[]{:S(2)}) collective-permute-start(bf16[128,640]{1,0:T(8,128)(2,1)S(1)} %collective-permute-done.13), channel_id=1, source_target_pairs={{16,0},{32,16},{48,32},{64,48},{80,64},{96,80},{112,96},{128,112},... | collective-permute-start | bytes 491528 | tf_op jit(solution)/shard_map/ppermute | solution.py:26
  59.3 0.7 bitcast_dynamic-update-slice_fusion.15
  60.0 0.7 bitcast_dynamic-update-slice_fusion.14
  60.7 0.7 bitcast_dynamic-update-slice_fusion.13
  61.3 0.7 bitcast_dynamic-update-slice_fusion.12
  62.0 0.7 bitcast_dynamic-update-slice_fusion.11
  62.7 0.7 bitcast_dynamic-update-slice_fusion.10
  63.4 0.7 bitcast_dynamic-update-slice_fusion.9
  64.1 0.7 bitcast_dynamic-update-slice_fusion.8
  64.8 0.7 bitcast_dynamic-update-slice_fusion.7
  65.4 0.7 bitcast_dynamic-update-slice_fusion.6
  66.1 0.7 bitcast_dynamic-update-slice_fusion.5
  66.8 0.7 bitcast_dynamic-update-slice_fusion.4
  67.5 0.7 bitcast_dynamic-update-slice_fusion.3
  68.2 0.7 bitcast_dynamic-update-slice_fusion.2
  68.8 0.7 bitcast_dynamic-update-slice_fusion.1
  69.5 0.7 bitcast_dynamic-update-slice_fusion
  70.2 2.8 %gather_fusion = bf16[16,128,640]{2,1,0:T(8,128)(2,1)S(1)} fusion(bf16[16,128,640]{2,1,0:T(8,128)(2,1)} %bitcast_dynamic-update-slice_fusion, s32[1024]{0:T(1024)S(1)} %pad_clamp_fusion), kind=kCustom, calls=%fused_computation | custom fusion | bytes 5242944 | tf_op jit(solution)/shard_map/gather | solution.py:29
  73.0 3.8 %fusion.60 = (bf16[512,512]{1,0:T(8,128)(2,1)S(1)}, f32[512,512]{1,0:T(8,128)}) fusion(bf16[512,2048]{1,0:T(8,128)(2,1)} %bitcast.18, bf16[2048,640]{1,0:T(8,128)(2,1)S(1)} %bitcast.145), kind=kOutput, calls=%fused_computation.119 | convolution fusion | flops 1074003968 | bytes 5767168 | tf_op jit(solution)/shard_map/dot_general | solution.py:79
  76.8 0.8 copy-done.2
  77.6 0.3 fusion.18
  78.1 0.9 broadcast_in_dim.123
  79.0 6.2 %all-to-all-start.1 = ((bf16[16,1,136,128]{3,2,1,0:T(8,128)(2,1)}), bf16[16,1,136,128]{3,2,1,0:T(8,128)(2,1)S(1)}, u32[]{:S(2)}, u32[]{:S(2)}) async-start(bf16[16,1,136,128]{3,2,1,0:T(8,128)(2,1)} %broadcast_in_dim.123), calls=%async_computation.1 | async-start | bytes 1114112 | tf_op jit(solution)/shard_map/all_to_all | solution.py:36
  85.3 0.8 copy-done
  86.2 1.4 %collective-permute-start.18 = (bf16[8,128,128]{2,1,0:T(8,128)(2,1)S(1)}, bf16[8,128,128]{2,1,0:T(8,128)(2,1)S(1)}, u32[]{:S(2)}, u32[]{:S(2)}) collective-permute-start(bf16[8,128,128]{2,1,0:T(8,128)(2,1)S(1)} %constant_dynamic-slice_fusion), channel_id=1, source_target_pairs={{0,2},{1,3},{2,0},{3,1},{4,6},{5,7},{6,4},{7,5},{8,10},{9,11},{10,... | collective-permute-start | bytes 786440 | tf_op jit(solution)/shard_map/ppermute | solution.py:155
  87.6 2.2 %collective-permute-start.19 = (bf16[8,128,128]{2,1,0:T(8,128)(2,1)S(1)}, bf16[8,128,128]{2,1,0:T(8,128)(2,1)S(1)}, u32[]{:S(2)}, u32[]{:S(2)}) collective-permute-start(bf16[8,128,128]{2,1,0:T(8,128)(2,1)S(1)} %constant_dynamic-slice_fusion), channel_id=1, source_target_pairs={{0,1},{1,2},{2,3},{3,0},{4,5},{5,6},{6,7},{7,4},{8,9},{9,10},{10,1... | collective-permute-start | bytes 786440 | tf_op jit(solution)/shard_map/ppermute | solution.py:155
  89.8 0.6 slice.69
  90.4 0.6 slice.68
  92.3 4.7 %collective-permute-done.18 = bf16[8,128,128]{2,1,0:T(8,128)(2,1)S(1)} collective-permute-done((bf16[8,128,128]{2,1,0:T(8,128)(2,1)S(1)}, bf16[8,128,128]{2,1,0:T(8,128)(2,1)S(1)}, u32[]{:S(2)}, u32[]{:S(2)}) %collective-permute-start.18) | collective-permute-done | bytes 262176 | tf_op jit(solution)/shard_map/ppermute | solution.py:155
  96.9 2.8 %collective-permute-done.19 = bf16[8,128,128]{2,1,0:T(8,128)(2,1)S(1)} collective-permute-done((bf16[8,128,128]{2,1,0:T(8,128)(2,1)S(1)}, bf16[8,128,128]{2,1,0:T(8,128)(2,1)S(1)}, u32[]{:S(2)}, u32[]{:S(2)}) %collective-permute-start.19) | collective-permute-done | bytes 262176 | tf_op jit(solution)/shard_map/ppermute | solution.py:155
  99.8 2.2 %collective-permute-done.20 = bf16[8,128,128]{2,1,0:T(8,128)(2,1)S(1)} collective-permute-done((bf16[8,128,128]{2,1,0:T(8,128)(2,1)S(1)}, bf16[8,128,128]{2,1,0:T(8,128)(2,1)S(1)}, u32[]{:S(2)}, u32[]{:S(2)}) %collective-permute-start.20) | collective-permute-done | bytes 262176 | tf_op jit(solution)/shard_map/ppermute | solution.py:155
  102.2 1.6 %fusion.15 = f32[1,512,1,128]{3,1,2,0:T(8,128)S(1)} fusion(f32[512]{0:T(512)S(1)} %get-tuple-element.22, bf16[512,512]{1,0:T(8,128)(2,1)} %copy-done.2), kind=kOutput, calls=%fused_computation.17 | convolution fusion | flops 135528448 | bytes 659456 | tf_op jit(solution)/shard_map/while/body/eval_jaxpr/hts,shd->thd/dot_general | solution.py:111
  104.3 1.5 %fusion.61 = (f32[512]{0:T(512)S(1)}, f32[1,512,1,128]{3,1,2,0:T(8,128)S(1)}) fusion(f32[1,512,1,128]{3,1,2,0:T(8,128)S(1)} %fusion.15, f32[512]{0:T(512)S(1)} %exp.53, bf16[512,512]{1,0:T(8,128)(2,1)} %copy-done.2, f32[128,128]{1,0:T(8,128)S(1)} %multiply_reduce_fusion, f32[]{:T(128)} %bitcast.29), kind=kOutput, calls=%fused_computation.120 | convolution fusion | flops 100941312 | bytes 725504 | tf_op jit(solution)/shard_map/cthd,chde->cthe/dot_general | solution.py:128
  106.0 1.2 fusion.32
  107.2 1.6 %collective-permute-start.15 = (bf16[4,32,128]{2,1,0:T(8,128)(2,1)S(1)}, bf16[4,32,128]{2,1,0:T(8,128)(2,1)S(1)}, u32[]{:S(2)}, u32[]{:S(2)}) collective-permute-start(bf16[4,32,128]{2,1,0:T(8,128)(2,1)S(1)} %get-tuple-element.42), channel_id=1, source_target_pairs={{0,2},{1,3},{2,0},{3,1},{4,6},{5,7},{6,4},{7,5},{8,10},{9,11},{10,... | collective-permute-start | bytes 98312 | tf_op jit(solution)/shard_map/ppermute | solution.py:154
  108.8 1.1 collective-permute-start.16
  109.9 0.9 collective-permute-start.17
  111.0 1.7 %collective-permute-done.15 = bf16[4,32,128]{2,1,0:T(8,128)(2,1)S(1)} collective-permute-done((bf16[4,32,128]{2,1,0:T(8,128)(2,1)S(1)}, bf16[4,32,128]{2,1,0:T(8,128)(2,1)S(1)}, u32[]{:S(2)}, u32[]{:S(2)}) %collective-permute-start.15) | collective-permute-done | bytes 32800 | tf_op jit(solution)/shard_map/ppermute | solution.py:154
  112.7 2.3 %collective-permute-done.17 = bf16[4,32,128]{2,1,0:T(8,128)(2,1)S(1)} collective-permute-done((bf16[4,32,128]{2,1,0:T(8,128)(2,1)S(1)}, bf16[4,32,128]{2,1,0:T(8,128)(2,1)S(1)}, u32[]{:S(2)}, u32[]{:S(2)}) %collective-permute-start.17) | collective-permute-done | bytes 32800 | tf_op jit(solution)/shard_map/ppermute | solution.py:154
  115.1 0.5 fusion.13
  115.7 3.1 %collective-permute-start.22 = (bf16[32,2048]{1,0:T(8,128)(2,1)S(1)}, bf16[32,2048]{1,0:T(8,128)(2,1)S(1)}, u32[]{:S(2)}, u32[]{:S(2)}) collective-permute-start(bf16[32,2048]{1,0:T(8,128)(2,1)S(1)} %get-tuple-element.25), channel_id=1, source_target_pairs={{0,8},{1,9},{2,10},{3,11},{4,12},{5,13},{6,14},{7,15},{8,0},{9,1},... | collective-permute-start | bytes 393224 | tf_op jit(solution)/shard_map/ppermute | solution.py:173
  118.7 0.6 collective-permute-start.23
  119.3 2.6 %collective-permute-start.24 = (bf16[32,2048]{1,0:T(8,128)(2,1)S(1)}, bf16[32,2048]{1,0:T(8,128)(2,1)S(1)}, u32[]{:S(2)}, u32[]{:S(2)}) collective-permute-start(bf16[32,2048]{1,0:T(8,128)(2,1)S(1)} %get-tuple-element.26), channel_id=1, source_target_pairs={{0,12},{1,13},{2,14},{3,15},{4,0},{5,1},{6,2},{7,3},{8,4},{9,5},{1... | collective-permute-start | bytes 393224 | tf_op jit(solution)/shard_map/ppermute | solution.py:173
  122.0 1.4 %collective-permute-done.22 = bf16[32,2048]{1,0:T(8,128)(2,1)S(1)} collective-permute-done((bf16[32,2048]{1,0:T(8,128)(2,1)S(1)}, bf16[32,2048]{1,0:T(8,128)(2,1)S(1)}, u32[]{:S(2)}, u32[]{:S(2)}) %collective-permute-start.22) | collective-permute-done | bytes 131104 | tf_op jit(solution)/shard_map/ppermute | solution.py:173
  123.4 1.7 %collective-permute-done.23 = bf16[32,2048]{1,0:T(8,128)(2,1)S(1)} collective-permute-done((bf16[32,2048]{1,0:T(8,128)(2,1)S(1)}, bf16[32,2048]{1,0:T(8,128)(2,1)S(1)}, u32[]{:S(2)}, u32[]{:S(2)}) %collective-permute-start.23) | collective-permute-done | bytes 131104 | tf_op jit(solution)/shard_map/ppermute | solution.py:173
  125.1 0.7 fusion.27
  (61 shorter events, 2.8 us)
Async XLA Ops:
  0.9 8.3 %collective-permute-start = (bf16[128,640]{1,0:T(8,128)(2,1)S(1)}, bf16[128,640]{1,0:T(8,128)(2,1)S(1)}, u32[]{:S(2)}, u32[]{:S(2)}) collective-permute-start(bf16[128,640]{1,0:T(8,128)(2,1)S(1)} %select_select_fusion), channel_id=1, source_target_pairs={{0,16},{16,32},{32,48},{48,64},{64,80},{80,96},{96,112},{112,128},... | collective-permute-start | bytes 491528 | tf_op jit(solution)/shard_map/ppermute | solution.py:24
  9.2 6.0 %collective-permute-start.1 = (bf16[128,640]{1,0:T(8,128)(2,1)S(1)}, bf16[128,640]{1,0:T(8,128)(2,1)S(1)}, u32[]{:S(2)}, u32[]{:S(2)}) collective-permute-start(bf16[128,640]{1,0:T(8,128)(2,1)S(1)} %collective-permute-done), channel_id=1, source_target_pairs={{0,16},{16,32},{32,48},{48,64},{64,80},{80,96},{96,112},{112,128},... | collective-permute-start | bytes 491528 | tf_op jit(solution)/shard_map/ppermute | solution.py:24
  9.2 6.0 %collective-permute-start.8 = (bf16[128,640]{1,0:T(8,128)(2,1)S(1)}, bf16[128,640]{1,0:T(8,128)(2,1)S(1)}, u32[]{:S(2)}, u32[]{:S(2)}) collective-permute-start(bf16[128,640]{1,0:T(8,128)(2,1)S(1)} %select_select_fusion), channel_id=1, source_target_pairs={{16,0},{32,16},{48,32},{64,48},{80,64},{96,80},{112,96},{128,112},... | collective-permute-start | bytes 491528 | tf_op jit(solution)/shard_map/ppermute | solution.py:26
  15.2 6.0 %collective-permute-start.2 = (bf16[128,640]{1,0:T(8,128)(2,1)S(1)}, bf16[128,640]{1,0:T(8,128)(2,1)S(1)}, u32[]{:S(2)}, u32[]{:S(2)}) collective-permute-start(bf16[128,640]{1,0:T(8,128)(2,1)S(1)} %collective-permute-done.1), channel_id=1, source_target_pairs={{0,16},{16,32},{32,48},{48,64},{64,80},{80,96},{96,112},{112,128},... | collective-permute-start | bytes 491528 | tf_op jit(solution)/shard_map/ppermute | solution.py:24
  15.2 6.0 %collective-permute-start.9 = (bf16[128,640]{1,0:T(8,128)(2,1)S(1)}, bf16[128,640]{1,0:T(8,128)(2,1)S(1)}, u32[]{:S(2)}, u32[]{:S(2)}) collective-permute-start(bf16[128,640]{1,0:T(8,128)(2,1)S(1)} %collective-permute-done.8), channel_id=1, source_target_pairs={{16,0},{32,16},{48,32},{64,48},{80,64},{96,80},{112,96},{128,112},... | collective-permute-start | bytes 491528 | tf_op jit(solution)/shard_map/ppermute | solution.py:26
  21.1 6.0 %collective-permute-start.3 = (bf16[128,640]{1,0:T(8,128)(2,1)S(1)}, bf16[128,640]{1,0:T(8,128)(2,1)S(1)}, u32[]{:S(2)}, u32[]{:S(2)}) collective-permute-start(bf16[128,640]{1,0:T(8,128)(2,1)S(1)} %collective-permute-done.2), channel_id=1, source_target_pairs={{0,16},{16,32},{32,48},{48,64},{64,80},{80,96},{96,112},{112,128},... | collective-permute-start | bytes 491528 | tf_op jit(solution)/shard_map/ppermute | solution.py:24
  21.1 16.7 %collective-permute-start.10 = (bf16[128,640]{1,0:T(8,128)(2,1)S(1)}, bf16[128,640]{1,0:T(8,128)(2,1)S(1)}, u32[]{:S(2)}, u32[]{:S(2)}) collective-permute-start(bf16[128,640]{1,0:T(8,128)(2,1)S(1)} %collective-permute-done.9), channel_id=1, source_target_pairs={{16,0},{32,16},{48,32},{64,48},{80,64},{96,80},{112,96},{128,112},... | collective-permute-start | bytes 491528 | tf_op jit(solution)/shard_map/ppermute | solution.py:26
  27.1 13.2 %collective-permute-start.4 = (bf16[128,640]{1,0:T(8,128)(2,1)S(1)}, bf16[128,640]{1,0:T(8,128)(2,1)S(1)}, u32[]{:S(2)}, u32[]{:S(2)}) collective-permute-start(bf16[128,640]{1,0:T(8,128)(2,1)S(1)} %collective-permute-done.3), channel_id=1, source_target_pairs={{0,16},{16,32},{32,48},{48,64},{64,80},{80,96},{96,112},{112,128},... | collective-permute-start | bytes 491528 | tf_op jit(solution)/shard_map/ppermute | solution.py:24
  29.6 7.6 %copy-start.3 = (f32[512,1]{0,1:T(1,128)S(1)}, f32[512,1]{0,1:T(1,128)}, u32[]{:S(2)}) copy-start(f32[512,1]{0,1:T(1,128)} %param.8) | copy-start | bytes 6148
  29.6 43.4 %all-to-all-start = ((bf16[16,32,2048]{2,1,0:T(8,128)(2,1)}), bf16[16,32,2048]{2,1,0:T(8,128)(2,1)}, u32[]{:S(2)}, u32[]{:S(2)}) async-start(bf16[16,32,2048]{2,1,0:T(8,128)(2,1)} %broadcast_in_dim.114), calls=%async_computation | async-start | bytes 4194304 | tf_op jit(solution)/shard_map/all_to_all | solution.py:36
  37.9 5.2 %collective-permute-start.11 = (bf16[128,640]{1,0:T(8,128)(2,1)S(1)}, bf16[128,640]{1,0:T(8,128)(2,1)S(1)}, u32[]{:S(2)}, u32[]{:S(2)}) collective-permute-start(bf16[128,640]{1,0:T(8,128)(2,1)S(1)} %collective-permute-done.10), channel_id=1, source_target_pairs={{16,0},{32,16},{48,32},{64,48},{80,64},{96,80},{112,96},{128,112},... | collective-permute-start | bytes 491528 | tf_op jit(solution)/shard_map/ppermute | solution.py:26
  40.2 6.4 %collective-permute-start.5 = (bf16[128,640]{1,0:T(8,128)(2,1)S(1)}, bf16[128,640]{1,0:T(8,128)(2,1)S(1)}, u32[]{:S(2)}, u32[]{:S(2)}) collective-permute-start(bf16[128,640]{1,0:T(8,128)(2,1)S(1)} %collective-permute-done.4), channel_id=1, source_target_pairs={{0,16},{16,32},{32,48},{48,64},{64,80},{80,96},{96,112},{112,128},... | collective-permute-start | bytes 491528 | tf_op jit(solution)/shard_map/ppermute | solution.py:24
  43.1 6.4 %collective-permute-start.12 = (bf16[128,640]{1,0:T(8,128)(2,1)S(1)}, bf16[128,640]{1,0:T(8,128)(2,1)S(1)}, u32[]{:S(2)}, u32[]{:S(2)}) collective-permute-start(bf16[128,640]{1,0:T(8,128)(2,1)S(1)} %collective-permute-done.11), channel_id=1, source_target_pairs={{16,0},{32,16},{48,32},{64,48},{80,64},{96,80},{112,96},{128,112},... | collective-permute-start | bytes 491528 | tf_op jit(solution)/shard_map/ppermute | solution.py:26
  46.6 6.4 %collective-permute-start.6 = (bf16[128,640]{1,0:T(8,128)(2,1)S(1)}, bf16[128,640]{1,0:T(8,128)(2,1)S(1)}, u32[]{:S(2)}, u32[]{:S(2)}) collective-permute-start(bf16[128,640]{1,0:T(8,128)(2,1)S(1)} %collective-permute-done.5), channel_id=1, source_target_pairs={{0,16},{16,32},{32,48},{48,64},{64,80},{80,96},{96,112},{112,128},... | collective-permute-start | bytes 491528 | tf_op jit(solution)/shard_map/ppermute | solution.py:24
  49.4 6.4 %collective-permute-start.13 = (bf16[128,640]{1,0:T(8,128)(2,1)S(1)}, bf16[128,640]{1,0:T(8,128)(2,1)S(1)}, u32[]{:S(2)}, u32[]{:S(2)}) collective-permute-start(bf16[128,640]{1,0:T(8,128)(2,1)S(1)} %collective-permute-done.12), channel_id=1, source_target_pairs={{16,0},{32,16},{48,32},{64,48},{80,64},{96,80},{112,96},{128,112},... | collective-permute-start | bytes 491528 | tf_op jit(solution)/shard_map/ppermute | solution.py:26
  53.0 6.4 %collective-permute-start.7 = (bf16[128,640]{1,0:T(8,128)(2,1)S(1)}, bf16[128,640]{1,0:T(8,128)(2,1)S(1)}, u32[]{:S(2)}, u32[]{:S(2)}) collective-permute-start(bf16[128,640]{1,0:T(8,128)(2,1)S(1)} %collective-permute-done.6), channel_id=1, source_target_pairs={{0,16},{16,32},{32,48},{48,64},{64,80},{80,96},{96,112},{112,128},... | collective-permute-start | bytes 491528 | tf_op jit(solution)/shard_map/ppermute | solution.py:24
  55.8 13.7 %collective-permute-start.14 = (bf16[128,640]{1,0:T(8,128)(2,1)S(1)}, bf16[128,640]{1,0:T(8,128)(2,1)S(1)}, u32[]{:S(2)}, u32[]{:S(2)}) collective-permute-start(bf16[128,640]{1,0:T(8,128)(2,1)S(1)} %collective-permute-done.13), channel_id=1, source_target_pairs={{16,0},{32,16},{48,32},{64,48},{80,64},{96,80},{112,96},{128,112},... | collective-permute-start | bytes 491528 | tf_op jit(solution)/shard_map/ppermute | solution.py:26
  76.8 0.8 copy-start.2
  79.0 24.7 %all-to-all-start.1 = ((bf16[16,1,136,128]{3,2,1,0:T(8,128)(2,1)}), bf16[16,1,136,128]{3,2,1,0:T(8,128)(2,1)S(1)}, u32[]{:S(2)}, u32[]{:S(2)}) async-start(bf16[16,1,136,128]{3,2,1,0:T(8,128)(2,1)} %broadcast_in_dim.123), calls=%async_computation.1 | async-start | bytes 1114112 | tf_op jit(solution)/shard_map/all_to_all | solution.py:36
  85.3 0.8 copy-start
  86.2 10.8 %collective-permute-start.18 = (bf16[8,128,128]{2,1,0:T(8,128)(2,1)S(1)}, bf16[8,128,128]{2,1,0:T(8,128)(2,1)S(1)}, u32[]{:S(2)}, u32[]{:S(2)}) collective-permute-start(bf16[8,128,128]{2,1,0:T(8,128)(2,1)S(1)} %constant_dynamic-slice_fusion), channel_id=1, source_target_pairs={{0,2},{1,3},{2,0},{3,1},{4,6},{5,7},{6,4},{7,5},{8,10},{9,11},{10,... | collective-permute-start | bytes 786440 | tf_op jit(solution)/shard_map/ppermute | solution.py:155
  87.6 12.2 %collective-permute-start.19 = (bf16[8,128,128]{2,1,0:T(8,128)(2,1)S(1)}, bf16[8,128,128]{2,1,0:T(8,128)(2,1)S(1)}, u32[]{:S(2)}, u32[]{:S(2)}) collective-permute-start(bf16[8,128,128]{2,1,0:T(8,128)(2,1)S(1)} %constant_dynamic-slice_fusion), channel_id=1, source_target_pairs={{0,1},{1,2},{2,3},{3,0},{4,5},{5,6},{6,7},{7,4},{8,9},{9,10},{10,1... | collective-permute-start | bytes 786440 | tf_op jit(solution)/shard_map/ppermute | solution.py:155
  89.8 12.2 %collective-permute-start.20 = (bf16[8,128,128]{2,1,0:T(8,128)(2,1)S(1)}, bf16[8,128,128]{2,1,0:T(8,128)(2,1)S(1)}, u32[]{:S(2)}, u32[]{:S(2)}) collective-permute-start(bf16[8,128,128]{2,1,0:T(8,128)(2,1)S(1)} %constant_dynamic-slice_fusion), channel_id=1, source_target_pairs={{0,3},{1,0},{2,1},{3,2},{4,7},{5,4},{6,5},{7,6},{8,11},{9,8},{10,9... | collective-permute-start | bytes 786440 | tf_op jit(solution)/shard_map/ppermute | solution.py:155
  102.1 8.8 %collective-permute-start.21 = (bf16[3,8,128,128]{3,2,0,1:T(8,128)(2,1)S(1)}, bf16[3,8,128,128]{3,2,0,1:T(8,128)(2,1)S(1)}, u32[]{:S(2)}, u32[]{:S(2)}) collective-permute-start(bf16[3,8,128,128]{3,2,0,1:T(8,128)(2,1)S(1)} %pad_maximum_fusion), channel_id=1, source_target_pairs={{0,16},{16,0},{32,48},{48,32},{64,80},{80,64},{96,112},{112,96},{1... | collective-permute-start | bytes 2359304 | tf_op jit(solution)/shard_map/ppermute | solution.py:157
  104.3 10.8 %copy-start.1 = (bf16[2048,128]{1,0:T(8,128)(2,1)S(1)}, bf16[2048,128]{1,0:T(8,128)(2,1)}, u32[]{:S(2)}) copy-start(bf16[2048,128]{1,0:T(8,128)(2,1)} %copy-done) | copy-start | bytes 1572868
  107.2 5.5 %collective-permute-start.15 = (bf16[4,32,128]{2,1,0:T(8,128)(2,1)S(1)}, bf16[4,32,128]{2,1,0:T(8,128)(2,1)S(1)}, u32[]{:S(2)}, u32[]{:S(2)}) collective-permute-start(bf16[4,32,128]{2,1,0:T(8,128)(2,1)S(1)} %get-tuple-element.42), channel_id=1, source_target_pairs={{0,2},{1,3},{2,0},{3,1},{4,6},{5,7},{6,4},{7,5},{8,10},{9,11},{10,... | collective-permute-start | bytes 98312 | tf_op jit(solution)/shard_map/ppermute | solution.py:154
  108.8 3.9 %collective-permute-start.16 = (bf16[4,32,128]{2,1,0:T(8,128)(2,1)S(1)}, bf16[4,32,128]{2,1,0:T(8,128)(2,1)S(1)}, u32[]{:S(2)}, u32[]{:S(2)}) collective-permute-start(bf16[4,32,128]{2,1,0:T(8,128)(2,1)S(1)} %get-tuple-element.41), channel_id=1, source_target_pairs={{0,1},{1,2},{2,3},{3,0},{4,5},{5,6},{6,7},{7,4},{8,9},{9,10},{10,1... | collective-permute-start | bytes 98312 | tf_op jit(solution)/shard_map/ppermute | solution.py:154
  109.9 5.1 %collective-permute-start.17 = (bf16[4,32,128]{2,1,0:T(8,128)(2,1)S(1)}, bf16[4,32,128]{2,1,0:T(8,128)(2,1)S(1)}, u32[]{:S(2)}, u32[]{:S(2)}) collective-permute-start(bf16[4,32,128]{2,1,0:T(8,128)(2,1)S(1)} %get-tuple-element.40), channel_id=1, source_target_pairs={{0,3},{1,0},{2,1},{3,2},{4,7},{5,4},{6,5},{7,6},{8,11},{9,8},{10,9... | collective-permute-start | bytes 98312 | tf_op jit(solution)/shard_map/ppermute | solution.py:154
  115.7 7.7 %collective-permute-start.22 = (bf16[32,2048]{1,0:T(8,128)(2,1)S(1)}, bf16[32,2048]{1,0:T(8,128)(2,1)S(1)}, u32[]{:S(2)}, u32[]{:S(2)}) collective-permute-start(bf16[32,2048]{1,0:T(8,128)(2,1)S(1)} %get-tuple-element.25), channel_id=1, source_target_pairs={{0,8},{1,9},{2,10},{3,11},{4,12},{5,13},{6,14},{7,15},{8,0},{9,1},... | collective-permute-start | bytes 393224 | tf_op jit(solution)/shard_map/ppermute | solution.py:173
  118.7 6.4 %collective-permute-start.23 = (bf16[32,2048]{1,0:T(8,128)(2,1)S(1)}, bf16[32,2048]{1,0:T(8,128)(2,1)S(1)}, u32[]{:S(2)}, u32[]{:S(2)}) collective-permute-start(bf16[32,2048]{1,0:T(8,128)(2,1)S(1)} %get-tuple-element.36), channel_id=1, source_target_pairs={{0,4},{1,5},{2,6},{3,7},{4,8},{5,9},{6,10},{7,11},{8,12},{9,13},{1... | collective-permute-start | bytes 393224 | tf_op jit(solution)/shard_map/ppermute | solution.py:173
  119.3 5.8 %collective-permute-start.24 = (bf16[32,2048]{1,0:T(8,128)(2,1)S(1)}, bf16[32,2048]{1,0:T(8,128)(2,1)S(1)}, u32[]{:S(2)}, u32[]{:S(2)}) collective-permute-start(bf16[32,2048]{1,0:T(8,128)(2,1)S(1)} %get-tuple-element.26), channel_id=1, source_target_pairs={{0,12},{1,13},{2,14},{3,15},{4,0},{5,1},{6,2},{7,3},{8,4},{9,5},{1... | collective-permute-start | bytes 393224 | tf_op jit(solution)/shard_map/ppermute | solution.py:173
